TPU v7x, 512 devices: a whole 4x4x16 slice. The times are simulated.
512 devices in a mesh: seq: 256 (over z, y, x), head: 2 (over core).
Axes of the slice: x: 4, y: 4, z: 16, core: 2. Of those that a mesh axis runs over, the one named last changes fastest.
Arguments:
- queries: bfloat16 [131072, 1024], P('seq', 'head'), may hold values from -12 to 12
- key_states: bfloat16 [131072, 1024], P('seq', 'head'), may hold values from -5 to 5
- value_states: bfloat16 [131072, 1024], P('seq', 'head'), may hold values from -6 to 6
- out_grad: bfloat16 [131072, 1024], P('seq', 'head'), may hold values from -6 to 6
Outputs:
- normalized: bfloat16 [131072, 1024], P('seq', 'head')
- grad_queries: bfloat16 [131072, 1024], P('seq', 'head')
- grad_keys: bfloat16 [131072, 1024], P('seq', 'head')
- grad_values: bfloat16 [131072, 1024], P('seq', 'head')
All inputs are finite; a program needn't handle non-finite values.
Results may differ from a plain program's by a relative error of at most 0.035.
Values may be sent and summed in bfloat16 or wider, within the bound.
No kernel may reach another device: no remote copies, remote signals or barrier semaphores. Data moves between devices by JAX's collectives and lax.ppermute only.
A program may use at most 64 MiB of HBM per device.

v0:
```python
import jax
import jax.numpy as jnp
from jax import lax
from jax.experimental import pallas as pl
from jax.experimental.pallas import tpu as pltpu
from jax.sharding import PartitionSpec as P


DH = 128
EPSILON = 1e-06
SCALE = DH ** (-0.5)
F32 = jnp.float32
BF16 = jnp.bfloat16


def from_partner(value, mask):
    pairs = [(source, source ^ mask) for source in range(lax.axis_size("seq"))]
    return lax.ppermute(value, "seq", pairs)


def _nt(a, b):
    return lax.dot_general(a, b, (((1,), (1,)), ((), ())), preferred_element_type=F32)


def _nn(a, b):
    return lax.dot_general(a, b, (((1,), (0,)), ((), ())), preferred_element_type=F32)


def _tn(a, b):
    return lax.dot_general(a, b, (((0,), (0,)), ((), ())), preferred_element_type=F32)


def _lanes(shape):
    return lax.broadcasted_iota(jnp.int32, shape, len(shape) - 1)


def _halve_kernel(q0, k0, v0, s1_ref, q1_ref, s2_ref, q2_ref, wide, half):
    n1 = half.shape[0]
    n2 = n1 // 2
    for h in range(q0.shape[1] // DH):
        cols = slice(h * DH, (h + 1) * DH)
        for i, src in enumerate((k0, v0, q0)):
            wide[...] = src[:, cols].astype(F32)
            h1 = ((wide[pl.ds(0, n1, stride=2), :] + wide[pl.ds(1, n1, stride=2), :]) * 0.5).astype(BF16)
            half[...] = h1.astype(F32)
            h2 = ((half[pl.ds(0, n2, stride=2), :] + half[pl.ds(1, n2, stride=2), :]) * 0.5).astype(BF16)
            if i < 2:
                s1_ref[i, :, cols] = h1
                s2_ref[i, :, cols] = h2
            else:
                q1_ref[:, cols] = h1
                q2_ref[:, cols] = h2


def _fwd0_kernel(q0, k0, v0, a0_ref, ms_ref):
    s = _nt(q0[...], k0[...]) * SCALE
    m = s.max(-1, keepdims=True)
    e = jnp.exp(s - m)
    a0_ref[...] = _nn(e.astype(BF16), v0[...])
    lane = _lanes(ms_ref.shape)
    ms_ref[...] = jnp.where(lane == 0, m, jnp.where(lane == 1, e.sum(-1, keepdims=True), 0.0))


def _fwd12_kernel(a0, ms0, g0, q1, k1p, v1p, q2, k2a, v2a, k2b, v2b,
                  att_ref, w_ref, sums_ref,
                  a1s, m1s, s1s, a2s, m2s, s2s, atts, ws):
    h = pl.program_id(0)
    n0 = atts.shape[0]
    n2 = a2s.shape[0]

    def put(a_ref, m_ref, s_ref, a, m, s):
        a_ref[...] = a
        m_ref[...] = jnp.broadcast_to(m, a.shape)
        s_ref[...] = jnp.broadcast_to(s, a.shape)

    s = _nt(q1[...], k1p[...]) * SCALE
    m = s.max(-1, keepdims=True)
    e = jnp.exp(s - m)
    put(a1s, m1s, s1s, _nn(e.astype(BF16), v1p[...]), m, e.sum(-1, keepdims=True))

    qv = q2[...]
    sa = _nt(qv, k2a[...]) * SCALE
    sb = _nt(qv, k2b[...]) * SCALE
    m = jnp.maximum(sa.max(-1, keepdims=True), sb.max(-1, keepdims=True))
    ea = jnp.exp(sa - m)
    eb = jnp.exp(sb - m)
    a = _nn(ea.astype(BF16), v2a[...]) + _nn(eb.astype(BF16), v2b[...])
    put(a2s, m2s, s2s, a, m, ea.sum(-1, keepdims=True) + eb.sum(-1, keepdims=True))

    lane = _lanes((n2, DH))
    for j in range(4):
        r0 = pl.ds(j, n2, stride=4)
        r1 = pl.ds(j >> 1, n2, stride=2)
        ms = ms0[r0, :]
        mm0 = ms[:, 0:1]
        mm1 = m1s[r1, :]
        mm2 = m2s[...]
        top = jnp.maximum(jnp.maximum(mm0, mm1), mm2)
        f0 = jnp.exp(mm0 - top)
        f1 = 2.0 * jnp.exp(mm1 - top)
        f2 = 4.0 * jnp.exp(mm2 - top)
        den = f0 * ms[:, 1:2] + f1 * s1s[r1, :] + f2 * s2s[...]
        num = f0 * a0[r0, :] + f1 * a1s[r1, :] + f2 * a2s[...]
        atts[r0, :] = (num / den).astype(BF16).astype(F32)
        ws[r0, :] = jnp.where(
            lane == 0, f0 / den, jnp.where(lane == 1, f1 / den, jnp.where(lane == 2, f2 / den, 0.0))
        )
    attv = atts[...]
    att_ref[...] = attv.astype(BF16)
    w_ref[...] = ws[...]
    gf = g0[...].astype(F32)
    sq = (attv * attv).sum(-1, keepdims=True)
    dt = (gf * attv).sum(-1, keepdims=True)
    lane0 = _lanes((n0, DH))
    part = jnp.where(lane0 == 0, sq, jnp.where(lane0 == 1, dt, 0.0))

    @pl.when(h == 0)
    def _():
        sums_ref[...] = part

    @pl.when(h > 0)
    def _():
        sums_ref[...] += part


def _level_grads(g0, att, w, mine, theirs, t_s, u_s):
    n0 = t_s.shape[0]
    n1 = n0 // 2
    n2 = n0 // 4
    full_width = 2 * 4 * DH
    totals = mine[:, 0:2] + theirs[:, 0:2]
    inv = lax.rsqrt(totals[:, 0:1] / full_width + EPSILON)
    coef = inv * inv * inv * totals[:, 1:2] / full_width
    attv = att[...].astype(F32)
    gf = g0[...].astype(F32)
    ga = inv * gf - coef * attv
    rt = (ga * attv).sum(-1, keepdims=True)
    wv = w[...]
    w0 = wv[:, 0:1]
    w1 = wv[:, 1:2]
    w2 = wv[:, 2:3]
    gl0 = (w0 * ga).astype(BF16)
    dl0 = w0 * rt
    t_s[...] = w1 * ga
    u_s[...] = jnp.broadcast_to(w1 * rt, (n0, DH))
    e_rows = pl.ds(0, n1, stride=2)
    o_rows = pl.ds(1, n1, stride=2)
    gl1 = (t_s[e_rows, :] + t_s[o_rows, :]).astype(BF16)
    dl1 = u_s[e_rows, :] + u_s[o_rows, :]
    t_s[...] = w2 * ga
    u_s[...] = jnp.broadcast_to(w2 * rt, (n0, DH))
    rows = [pl.ds(j, n2, stride=4) for j in range(4)]
    gl2 = (((t_s[rows[0], :] + t_s[rows[1], :]) + t_s[rows[2], :]) + t_s[rows[3], :]).astype(BF16)
    dl2 = ((u_s[rows[0], :] + u_s[rows[1], :]) + u_s[rows[2], :]) + u_s[rows[3], :]
    return inv, attv, gl0, dl0, gl1, dl1, gl2, dl2


def _split3(x):
    hi = x.astype(BF16).astype(F32)
    rest = x - hi
    mid = rest.astype(BF16).astype(F32)
    return hi, mid, rest - mid


def _coded(pieces):
    sub = lax.broadcasted_iota(jnp.int32, (16, DH), 0)
    out = jnp.zeros((16, DH), F32)
    for i, piece in enumerate(pieces):
        out = jnp.where(sub == i, piece, out)
    return out.astype(BF16)


def _bwd1_kernel(g0, att, w, mine, theirs, q1, q2, norm_ref, b1_ref, b2_ref, t_s, u_s):
    inv, attv, _, _, gl1, dl1, gl2, dl2 = _level_grads(g0, att, w, mine, theirs, t_s, u_s)
    n1 = gl1.shape[0]
    n2 = gl2.shape[0]
    norm_ref[...] = (attv * inv).astype(BF16)
    b1_ref[0:n1, :] = gl1
    b2_ref[0:n2, :] = gl2
    t1 = dl1.T
    a_parts = _split3(t1[0:1, 0:DH])
    b_parts = _split3(t1[0:1, DH:2 * DH])
    b1_ref[n1:n1 + 16, :] = _coded([a_parts[0], b_parts[0], a_parts[1], b_parts[1], a_parts[2], b_parts[2]])
    b2_ref[n2:n2 + 16, :] = _coded(list(_split3(dl2.T[0:1, :])))
    b1_ref[n1 + 16:, :] = q1[...]
    b2_ref[n2 + 16:, :] = q2[...]


def _bwd2_kernel(q0, k0, v0, g0, att, w, mine, theirs, q1, k1p, v1p, q2, k2a, v2a, k2b, v2b,
                 gq_ref, dk0_ref, dv0_ref,
                 t_s, u_s, dq0s, dq1s, dq2s, outs):
    n2 = dq2s.shape[0]
    _, _, gl0, dl0, gl1, dl1, gl2, dl2 = _level_grads(g0, att, w, mine, theirs, t_s, u_s)
    q0v = q0[...]
    k0v = k0[...]
    v0v = v0[...]
    s = _nt(q0v, k0v) * SCALE
    m = s.max(-1, keepdims=True)
    e = jnp.exp(s - m)
    p = e.astype(BF16)
    ds = (e * (_nt(gl0, v0v) - dl0)).astype(BF16)
    dq0s[...] = _nn(ds, k0v) * SCALE
    dk0_ref[...] = _tn(ds, q0v) * SCALE
    dv0_ref[...] = _tn(p, gl0)

    kv = k1p[...]
    s = _nt(q1[...], kv) * SCALE
    m = s.max(-1, keepdims=True)
    e = jnp.exp(s - m)
    ds = (e * (_nt(gl1, v1p[...]) - dl1[:, 0:1])).astype(BF16)
    dq1s[...] = _nn(ds, kv) * SCALE

    qv = q2[...]
    ka = k2a[...]
    kb = k2b[...]
    sa = _nt(qv, ka) * SCALE
    sb = _nt(qv, kb) * SCALE
    m = jnp.maximum(sa.max(-1, keepdims=True), sb.max(-1, keepdims=True))
    ea = jnp.exp(sa - m)
    eb = jnp.exp(sb - m)
    d2c = dl2[:, 0:1]
    dsa = (ea * (_nt(gl2, v2a[...]) - d2c)).astype(BF16)
    dsb = (eb * (_nt(gl2, v2b[...]) - d2c)).astype(BF16)
    dq2s[...] = (_nn(dsa, ka) + _nn(dsb, kb)) * SCALE

    for j in range(4):
        r0 = pl.ds(j, n2, stride=4)
        r1 = pl.ds(j >> 1, n2, stride=2)
        outs[r0, :] = dq0s[r0, :] + dq1s[r1, :] * 0.5 + dq2s[...] * 0.25
    gq_ref[...] = outs[...].astype(BF16)


def _own_kernel(k1o, v1o, k1p, b1p, k2o, v2o, b2a, b2b, dk0, dv0,
                gk_ref, gv_ref, wide, dk1s, dv1s, dk2s, dv2s, outk, outv):
    n1 = dk1s.shape[0]
    n2 = dk2s.shape[0]
    qv = b1p[n1 + 16:, :]
    gv = b1p[0:n1, :]
    x = b1p[n1:n1 + 16, :].astype(F32)
    d_row = jnp.concatenate([(x[0:1] + x[2:3]) + x[4:5], (x[1:2] + x[3:4]) + x[5:6]], axis=1)
    st = _nt(k1o[...], qv) * SCALE
    m = st.max(0, keepdims=True)
    e = jnp.exp(st - m)
    p = e.astype(BF16)
    ds = (e * (_nt(v1o[...], gv) - d_row)).astype(BF16)
    dk1s[...] = _nn(ds, qv) * SCALE
    dv1s[...] = _nn(p, gv)

    wide[...] = k1p[...].astype(F32)
    ks = ((wide[pl.ds(0, n2, stride=2), :] + wide[pl.ds(1, n2, stride=2), :]) * 0.5).astype(BF16)
    ko = k2o[...]
    vo = v2o[...]
    dks = []
    dvs = []
    for b_ref in (b2a, b2b):
        qv = b_ref[n2 + 16:, :]
        gv = b_ref[0:n2, :]
        x = b_ref[n2:n2 + 16, :].astype(F32)
        d_row = (x[0:1] + x[1:2]) + x[2:3]
        so = _nt(ko, qv) * SCALE
        ss = _nt(ks, qv) * SCALE
        m = jnp.maximum(so.max(0, keepdims=True), ss.max(0, keepdims=True))
        e = jnp.exp(so - m)
        p = e.astype(BF16)
        ds = (e * (_nt(vo, gv) - d_row)).astype(BF16)
        dks.append(_nn(ds, qv))
        dvs.append(_nn(p, gv))
    dk2s[...] = (dks[0] + dks[1]) * SCALE
    dv2s[...] = dvs[0] + dvs[1]

    for j in range(4):
        r0 = pl.ds(j, n2, stride=4)
        r1 = pl.ds(j >> 1, n2, stride=2)
        outk[r0, :] = dk0[r0, :] + dk1s[r1, :] * 0.5 + dk2s[...] * 0.25
        outv[r0, :] = dv0[r0, :] + dv1s[r1, :] * 0.5 + dv2s[...] * 0.25
    gk_ref[...] = outk[...].astype(BF16)
    gv_ref[...] = outv[...].astype(BF16)


def _cols(rows):
    return pl.BlockSpec((rows, DH), lambda h: (0, h))


def _stacked(rows, index):
    return pl.BlockSpec((None, rows, DH), lambda h: (index, 0, h))


def _per_head(rows, width):
    return pl.BlockSpec((None, rows, width), lambda h: (h, 0, 0))


def _whole(rows, width):
    return pl.BlockSpec((rows, width), lambda h: (0, 0))


def _params():
    return pltpu.CompilerParams(dimension_semantics=("arbitrary",))


def _full3(rows, width):
    return pl.BlockSpec((2, rows, width), lambda h: (0, 0, 0))


def shards(queries, key_states, value_states, out_grad):
    n0, width = queries.shape
    heads = width // DH
    n1 = n0 // 2
    n2 = n0 // 4
    q0, k0, v0, g0 = queries, key_states, value_states, out_grad
    s1, q1, s2, q2 = pl.pallas_call(
        _halve_kernel,
        grid=(1,),
        in_specs=[_whole(n0, width), _whole(n0, width), _whole(n0, width)],
        out_specs=[_full3(n1, width), _whole(n1, width), _full3(n2, width), _whole(n2, width)],
        out_shape=[
            jax.ShapeDtypeStruct((2, n1, width), BF16),
            jax.ShapeDtypeStruct((n1, width), BF16),
            jax.ShapeDtypeStruct((2, n2, width), BF16),
            jax.ShapeDtypeStruct((n2, width), BF16),
        ],
        scratch_shapes=[pltpu.VMEM((n0, DH), F32), pltpu.VMEM((n1, DH), F32)],
        compiler_params=_params(),
    )(q0, k0, v0)
    r1 = from_partner(s1, 1)
    r2a = from_partner(s2, 2)
    r2b = from_partner(s2, 3)

    a0, ms0 = pl.pallas_call(
        _fwd0_kernel,
        grid=(heads,),
        in_specs=[_cols(n0), _cols(n0), _cols(n0)],
        out_specs=[_cols(n0), _per_head(n0, DH)],
        out_shape=[
            jax.ShapeDtypeStruct((n0, width), F32),
            jax.ShapeDtypeStruct((heads, n0, DH), F32),
        ],
        compiler_params=_params(),
    )(q0, k0, v0)

    att, w, sums = pl.pallas_call(
        _fwd12_kernel,
        grid=(heads,),
        in_specs=[
            _cols(n0), _per_head(n0, DH), _cols(n0),
            _cols(n1), _stacked(n1, 0), _stacked(n1, 1),
            _cols(n2), _stacked(n2, 0), _stacked(n2, 1), _stacked(n2, 0), _stacked(n2, 1),
        ],
        out_specs=[_cols(n0), _per_head(n0, DH), _whole(n0, DH)],
        out_shape=[
            jax.ShapeDtypeStruct((n0, width), BF16),
            jax.ShapeDtypeStruct((heads, n0, DH), F32),
            jax.ShapeDtypeStruct((n0, DH), F32),
        ],
        scratch_shapes=[pltpu.VMEM((n, DH), F32) for n in (n1, n1, n1, n2, n2, n2, n0, n0)],
        compiler_params=_params(),
    )(a0, ms0, g0, q1, r1, r1, q2, r2a, r2a, r2b, r2b)

    assert width * lax.axis_size("head") == 2 * 4 * DH
    other = lax.ppermute(sums, "head", [(0, 1), (1, 0)])

    norm, b1, b2 = pl.pallas_call(
        _bwd1_kernel,
        grid=(heads,),
        in_specs=[_cols(n0), _cols(n0), _per_head(n0, DH), _whole(n0, DH), _whole(n0, DH), _cols(n1), _cols(n2)],
        out_specs=[_cols(n0), _cols(2 * n1 + 16), _cols(2 * n2 + 16)],
        out_shape=[
            jax.ShapeDtypeStruct((n0, width), BF16),
            jax.ShapeDtypeStruct((2 * n1 + 16, width), BF16),
            jax.ShapeDtypeStruct((2 * n2 + 16, width), BF16),
        ],
        scratch_shapes=[pltpu.VMEM((n0, DH), F32), pltpu.VMEM((n0, DH), F32)],
        compiler_params=_params(),
    )(g0, att, w, sums, other, q1, q2)
    b1p = from_partner(b1, 1)
    b2a = from_partner(b2, 2)
    b2b = from_partner(b2, 3)

    gq, dk0, dv0 = pl.pallas_call(
        _bwd2_kernel,
        grid=(heads,),
        in_specs=[
            _cols(n0), _cols(n0), _cols(n0), _cols(n0), _cols(n0), _per_head(n0, DH),
            _whole(n0, DH), _whole(n0, DH),
            _cols(n1), _stacked(n1, 0), _stacked(n1, 1),
            _cols(n2), _stacked(n2, 0), _stacked(n2, 1), _stacked(n2, 0), _stacked(n2, 1),
        ],
        out_specs=[_cols(n0), _cols(n0), _cols(n0)],
        out_shape=[
            jax.ShapeDtypeStruct((n0, width), BF16),
            jax.ShapeDtypeStruct((n0, width), F32),
            jax.ShapeDtypeStruct((n0, width), F32),
        ],
        scratch_shapes=[pltpu.VMEM((n, DH), F32) for n in (n0, n0, n0, n1, n2, n0)],
        compiler_params=_params(),
    )(q0, k0, v0, g0, att, w, sums, other, q1, r1, r1, q2, r2a, r2a, r2b, r2b)

    gk, gv = pl.pallas_call(
        _own_kernel,
        grid=(heads,),
        in_specs=[
            _stacked(n1, 0), _stacked(n1, 1), _stacked(n1, 0), _cols(2 * n1 + 16),
            _stacked(n2, 0), _stacked(n2, 1), _cols(2 * n2 + 16), _cols(2 * n2 + 16),
            _cols(n0), _cols(n0),
        ],
        out_specs=[_cols(n0), _cols(n0)],
        out_shape=[
            jax.ShapeDtypeStruct((n0, width), BF16),
            jax.ShapeDtypeStruct((n0, width), BF16),
        ],
        scratch_shapes=[pltpu.VMEM((n, DH), F32) for n in (n1, n1, n1, n2, n2, n0, n0)],
        compiler_params=_params(),
    )(s1, s1, r1, b1p, s2, s2, b2a, b2b, dk0, dv0)
    return (norm, gq, gk, gv)


def solution(mesh):
    return jax.shard_map(
        shards,
        mesh=mesh,
        in_specs=(P("seq", "head"), P("seq", "head"), P("seq", "head"), P("seq", "head")),
        out_specs=(P("seq", "head"), P("seq", "head"), P("seq", "head"), P("seq", "head")),
        check_vma=False,
    )
```

profile of v0, /device:TPU:1, one launch (start us, length us, event | category | flops | bytes accessed | tf_op | source)
XLA Modules:
  0.0 76.9 jit_solution(14831040571360207991)
XLA Ops:
  0.6 3.1 %shard_map.76 = (bf16[2,256,512]{2,1,0:T(8,128)(2,1)}, bf16[256,512]{1,0:T(8,128)(2,1)}, bf16[2,128,512]{2,1,0:T(8,128)(2,1)}, bf16[128,512]{1,0:T(8,128)(2,1)}) custom-call(bf16[512,512]{1,0:T(8,128)(2,1)} %q0.5, bf16[512,512]{1,0:T(8,128)(2,1)} %k0.5, bf16[512,512]{1,0:T(8,128)(2,1)} %v0.5), custom_call_target="tpu_custom_call" | custom-call | tf_op jit(solution)/shard_map/pallas_call | solution.py:310
  3.7 3.9 %collective-permute-start = (bf16[2,256,512]{2,1,0:T(8,128)(2,1)}, bf16[2,256,512]{2,1,0:T(8,128)(2,1)S(1)}, u32[]{:S(2)}, u32[]{:S(2)}) collective-permute-start(bf16[2,256,512]{2,1,0:T(8,128)(2,1)} %get-tuple-element.24.k1o.v1o), channel_id=1, source_target_pairs={{0,2},{2,0},{4,6},{6,4},{8,10},{10,8},{12,14},{14,12},{16,18},{18,... | collective-permute-start | bytes 1572872 | tf_op jit(solution)/shard_map/ppermute | solution.py:18
  7.7 4.4 %collective-permute-start.1 = (bf16[2,128,512]{2,1,0:T(8,128)(2,1)}, bf16[2,128,512]{2,1,0:T(8,128)(2,1)S(1)}, u32[]{:S(2)}, u32[]{:S(2)}) collective-permute-start(bf16[2,128,512]{2,1,0:T(8,128)(2,1)} %get-tuple-element.26.k2o.v2o), channel_id=1, source_target_pairs={{0,4},{2,6},{4,0},{6,2},{8,12},{10,14},{12,8},{14,10},{16,20},{18,... | collective-permute-start | bytes 786440 | tf_op jit(solution)/shard_map/ppermute | solution.py:18
  12.0 1.9 %collective-permute-start.2 = (bf16[2,128,512]{2,1,0:T(8,128)(2,1)}, bf16[2,128,512]{2,1,0:T(8,128)(2,1)S(1)}, u32[]{:S(2)}, u32[]{:S(2)}) collective-permute-start(bf16[2,128,512]{2,1,0:T(8,128)(2,1)} %get-tuple-element.26.k2o.v2o), channel_id=1, source_target_pairs={{0,6},{2,4},{4,2},{6,0},{8,14},{10,12},{12,10},{14,8},{16,22},{18,... | collective-permute-start | bytes 786440 | tf_op jit(solution)/shard_map/ppermute | solution.py:18
  14.0 5.4 %shard_map.75 = (f32[512,512]{1,0:T(8,128)}, f32[4,512,128]{2,1,0:T(8,128)}) custom-call(bf16[512,512]{1,0:T(8,128)(2,1)} %q0.5, bf16[512,512]{1,0:T(8,128)(2,1)} %k0.5, bf16[512,512]{1,0:T(8,128)(2,1)} %v0.5), custom_call_target="tpu_custom_call" | custom-call | tf_op jit(solution)/shard_map/pallas_call | solution.py:328
  19.4 7.9 %collective-permute-done.1.k2a.v2a = bf16[2,128,512]{2,1,0:T(8,128)(2,1)S(1)} collective-permute-done((bf16[2,128,512]{2,1,0:T(8,128)(2,1)}, bf16[2,128,512]{2,1,0:T(8,128)(2,1)S(1)}, u32[]{:S(2)}, u32[]{:S(2)}) %collective-permute-start.1) | collective-permute-done | bytes 262176 | tf_op jit(solution)/shard_map/ppermute | solution.py:18
  27.3 0.0 copy-start.1
  27.3 0.0 collective-permute-done.2.k2b.v2b
  27.3 0.0 copy-start.2
  27.3 0.0 collective-permute-done.k1p.v1p
  27.3 0.0 copy-start
  27.3 0.7 copy-done.1
  28.0 0.1 copy-done.2
  28.1 0.2 copy-done
  28.3 6.7 %shard_map.77 = (bf16[512,512]{1,0:T(8,128)(2,1)}, f32[4,512,128]{2,1,0:T(8,128)}, f32[512,128]{1,0:T(8,128)}) custom-call(f32[512,512]{1,0:T(8,128)} %get-tuple-element.21.a0, f32[4,512,128]{2,1,0:T(8,128)} %get-tuple-element.22.ms0, bf16[512,512]{1,0:T(8,128)(2,1)} %g0.5, bf16[256,512]{1,0:T(8,128)(2,1)} %get-tuple-element.23.q1, ...), custom_call_target="tpu_custom_call" | custom-call | tf_op jit(solution)/shard_map/pallas_call | solution.py:340
  35.0 5.3 %collective-permute-start.3 = (f32[512,128]{1,0:T(8,128)}, f32[512,128]{1,0:T(8,128)S(1)}, u32[]{:S(2)}, u32[]{:S(2)}) collective-permute-start(f32[512,128]{1,0:T(8,128)} %get-tuple-element.29.mine), channel_id=1, source_target_pairs={{0,1},{1,0},{2,3},{3,2},{4,5},{5,4},{6,7},{7,6},{8,9},{9,8},{10,11... | collective-permute-start | bytes 786440 | tf_op jit(solution)/shard_map/ppermute | solution.py:359
  40.4 1.4 %collective-permute-done.3.theirs = f32[512,128]{1,0:T(8,128)S(1)} collective-permute-done((f32[512,128]{1,0:T(8,128)}, f32[512,128]{1,0:T(8,128)S(1)}, u32[]{:S(2)}, u32[]{:S(2)}) %collective-permute-start.3) | collective-permute-done | bytes 262176 | tf_op jit(solution)/shard_map/ppermute | solution.py:359
  41.7 0.0 copy-start.3
  41.7 0.7 copy-done.3
  42.4 5.7 %shard_map.78 = (bf16[512,512]{1,0:T(8,128)(2,1)}, bf16[528,512]{1,0:T(8,128)(2,1)}, bf16[272,512]{1,0:T(8,128)(2,1)}) custom-call(bf16[512,512]{1,0:T(8,128)(2,1)} %g0.5, bf16[512,512]{1,0:T(8,128)(2,1)} %get-tuple-element.27.att, f32[4,512,128]{2,1,0:T(8,128)} %get-tuple-element.28.w, f32[512,128]{1,0:T(8,128)} %get-tuple-element.29.mine, ...), custom_call_target="tpu_custom_call" | custom-call | tf_op jit(solution)/shard_map/pallas_call | solution.py:361
  48.1 1.9 %collective-permute-start.4 = (bf16[528,512]{1,0:T(8,128)(2,1)}, bf16[528,512]{1,0:T(8,128)(2,1)S(1)}, u32[]{:S(2)}, u32[]{:S(2)}) collective-permute-start(bf16[528,512]{1,0:T(8,128)(2,1)} %get-tuple-element.32), channel_id=1, source_target_pairs={{0,2},{2,0},{4,6},{6,4},{8,10},{10,8},{12,14},{14,12},{16,18},{18,... | collective-permute-start | bytes 1622024 | tf_op jit(solution)/shard_map/ppermute | solution.py:18
  50.1 3.6 %collective-permute-start.5 = (bf16[272,512]{1,0:T(8,128)(2,1)}, bf16[272,512]{1,0:T(8,128)(2,1)S(1)}, u32[]{:S(2)}, u32[]{:S(2)}) collective-permute-start(bf16[272,512]{1,0:T(8,128)(2,1)} %get-tuple-element.33), channel_id=1, source_target_pairs={{0,4},{2,6},{4,0},{6,2},{8,12},{10,14},{12,8},{14,10},{16,20},{18,... | collective-permute-start | bytes 835592 | tf_op jit(solution)/shard_map/ppermute | solution.py:18
  53.6 4.1 %collective-permute-start.6 = (bf16[272,512]{1,0:T(8,128)(2,1)}, bf16[272,512]{1,0:T(8,128)(2,1)S(1)}, u32[]{:S(2)}, u32[]{:S(2)}) collective-permute-start(bf16[272,512]{1,0:T(8,128)(2,1)} %get-tuple-element.33), channel_id=1, source_target_pairs={{0,6},{2,4},{4,2},{6,0},{8,14},{10,12},{12,10},{14,8},{16,22},{18,... | collective-permute-start | bytes 835592 | tf_op jit(solution)/shard_map/ppermute | solution.py:18
  57.7 10.9 %shard_map.79 = (bf16[512,512]{1,0:T(8,128)(2,1)}, f32[512,512]{1,0:T(8,128)}, f32[512,512]{1,0:T(8,128)}) custom-call(bf16[512,512]{1,0:T(8,128)(2,1)} %q0.5, bf16[512,512]{1,0:T(8,128)(2,1)} %k0.5, bf16[512,512]{1,0:T(8,128)(2,1)} %v0.5, bf16[512,512]{1,0:T(8,128)(2,1)} %g0.5, bf16[512,512]{1,0:T(8,128)(2,1)} %get-tuple-element.27.att, ...), custom_call_target="tpu_custom_call" | custom-call | tf_op jit(solution)/shard_map/pallas_call | solution.py:378
  68.6 1.3 %collective-permute-done.5.b2a = bf16[272,512]{1,0:T(8,128)(2,1)S(1)} collective-permute-done((bf16[272,512]{1,0:T(8,128)(2,1)}, bf16[272,512]{1,0:T(8,128)(2,1)S(1)}, u32[]{:S(2)}, u32[]{:S(2)}) %collective-permute-start.5) | collective-permute-done | bytes 278560 | tf_op jit(solution)/shard_map/ppermute | solution.py:18
  69.9 0.0 copy-start.5
  69.9 0.0 collective-permute-done.6.b2b
  69.9 0.0 copy-start.6
  69.9 0.0 collective-permute-done.4.b1p
  69.9 0.0 copy-start.4
  69.9 0.7 copy-done.5
  70.6 0.1 copy-done.6
  70.7 0.2 copy-done.4
  70.9 6.0 %shard_map.80 = (bf16[512,512]{1,0:T(8,128)(2,1)}, bf16[512,512]{1,0:T(8,128)(2,1)}) custom-call(bf16[2,256,512]{2,1,0:T(8,128)(2,1)} %get-tuple-element.24.k1o.v1o, bf16[2,256,512]{2,1,0:T(8,128)(2,1)} %get-tuple-element.24.k1o.v1o, bf16[2,256,512]{2,1,0:T(8,128)(2,1)} %copy-done, bf16[528,512]{1,0:T(8,128)(2,1)} %copy-done.4, ...), custom_call_target="tpu_custom_call" | custom-call | tf_op jit(solution)/shard_map/pallas_call | solution.py:397
Async XLA Ops:
  3.7 23.6 %collective-permute-start = (bf16[2,256,512]{2,1,0:T(8,128)(2,1)}, bf16[2,256,512]{2,1,0:T(8,128)(2,1)S(1)}, u32[]{:S(2)}, u32[]{:S(2)}) collective-permute-start(bf16[2,256,512]{2,1,0:T(8,128)(2,1)} %get-tuple-element.24.k1o.v1o), channel_id=1, source_target_pairs={{0,2},{2,0},{4,6},{6,4},{8,10},{10,8},{12,14},{14,12},{16,18},{18,... | collective-permute-start | bytes 1572872 | tf_op jit(solution)/shard_map/ppermute | solution.py:18
  7.7 19.6 %collective-permute-start.1 = (bf16[2,128,512]{2,1,0:T(8,128)(2,1)}, bf16[2,128,512]{2,1,0:T(8,128)(2,1)S(1)}, u32[]{:S(2)}, u32[]{:S(2)}) collective-permute-start(bf16[2,128,512]{2,1,0:T(8,128)(2,1)} %get-tuple-element.26.k2o.v2o), channel_id=1, source_target_pairs={{0,4},{2,6},{4,0},{6,2},{8,12},{10,14},{12,8},{14,10},{16,20},{18,... | collective-permute-start | bytes 786440 | tf_op jit(solution)/shard_map/ppermute | solution.py:18
  12.0 15.3 %collective-permute-start.2 = (bf16[2,128,512]{2,1,0:T(8,128)(2,1)}, bf16[2,128,512]{2,1,0:T(8,128)(2,1)S(1)}, u32[]{:S(2)}, u32[]{:S(2)}) collective-permute-start(bf16[2,128,512]{2,1,0:T(8,128)(2,1)} %get-tuple-element.26.k2o.v2o), channel_id=1, source_target_pairs={{0,6},{2,4},{4,2},{6,0},{8,14},{10,12},{12,10},{14,8},{16,22},{18,... | collective-permute-start | bytes 786440 | tf_op jit(solution)/shard_map/ppermute | solution.py:18
  27.3 0.7 copy-start.1
  27.3 0.8 %copy-start.2 = (bf16[2,128,512]{2,1,0:T(8,128)(2,1)}, bf16[2,128,512]{2,1,0:T(8,128)(2,1)S(1)}, u32[]{:S(2)}) copy-start(bf16[2,128,512]{2,1,0:T(8,128)(2,1)S(1)} %collective-permute-done.2.k2b.v2b) | copy-start | bytes 786436
  27.3 1.0 %copy-start = (bf16[2,256,512]{2,1,0:T(8,128)(2,1)}, bf16[2,256,512]{2,1,0:T(8,128)(2,1)S(1)}, u32[]{:S(2)}) copy-start(bf16[2,256,512]{2,1,0:T(8,128)(2,1)S(1)} %collective-permute-done.k1p.v1p) | copy-start | bytes 1572868
  35.0 6.7 %collective-permute-start.3 = (f32[512,128]{1,0:T(8,128)}, f32[512,128]{1,0:T(8,128)S(1)}, u32[]{:S(2)}, u32[]{:S(2)}) collective-permute-start(f32[512,128]{1,0:T(8,128)} %get-tuple-element.29.mine), channel_id=1, source_target_pairs={{0,1},{1,0},{2,3},{3,2},{4,5},{5,4},{6,7},{7,6},{8,9},{9,8},{10,11... | collective-permute-start | bytes 786440 | tf_op jit(solution)/shard_map/ppermute | solution.py:359
  41.7 0.7 copy-start.3
  48.1 21.8 %collective-permute-start.4 = (bf16[528,512]{1,0:T(8,128)(2,1)}, bf16[528,512]{1,0:T(8,128)(2,1)S(1)}, u32[]{:S(2)}, u32[]{:S(2)}) collective-permute-start(bf16[528,512]{1,0:T(8,128)(2,1)} %get-tuple-element.32), channel_id=1, source_target_pairs={{0,2},{2,0},{4,6},{6,4},{8,10},{10,8},{12,14},{14,12},{16,18},{18,... | collective-permute-start | bytes 1622024 | tf_op jit(solution)/shard_map/ppermute | solution.py:18
  50.1 19.9 %collective-permute-start.5 = (bf16[272,512]{1,0:T(8,128)(2,1)}, bf16[272,512]{1,0:T(8,128)(2,1)S(1)}, u32[]{:S(2)}, u32[]{:S(2)}) collective-permute-start(bf16[272,512]{1,0:T(8,128)(2,1)} %get-tuple-element.33), channel_id=1, source_target_pairs={{0,4},{2,6},{4,0},{6,2},{8,12},{10,14},{12,8},{14,10},{16,20},{18,... | collective-permute-start | bytes 835592 | tf_op jit(solution)/shard_map/ppermute | solution.py:18
  53.6 16.3 %collective-permute-start.6 = (bf16[272,512]{1,0:T(8,128)(2,1)}, bf16[272,512]{1,0:T(8,128)(2,1)S(1)}, u32[]{:S(2)}, u32[]{:S(2)}) collective-permute-start(bf16[272,512]{1,0:T(8,128)(2,1)} %get-tuple-element.33), channel_id=1, source_target_pairs={{0,6},{2,4},{4,2},{6,0},{8,14},{10,12},{12,10},{14,8},{16,22},{18,... | collective-permute-start | bytes 835592 | tf_op jit(solution)/shard_map/ppermute | solution.py:18
  69.9 0.7 copy-start.5
  69.9 0.8 %copy-start.6 = (bf16[272,512]{1,0:T(8,128)(2,1)}, bf16[272,512]{1,0:T(8,128)(2,1)S(1)}, u32[]{:S(2)}) copy-start(bf16[272,512]{1,0:T(8,128)(2,1)S(1)} %collective-permute-done.6.b2b) | copy-start | bytes 835588
  69.9 1.0 %copy-start.4 = (bf16[528,512]{1,0:T(8,128)(2,1)}, bf16[528,512]{1,0:T(8,128)(2,1)S(1)}, u32[]{:S(2)}) copy-start(bf16[528,512]{1,0:T(8,128)(2,1)S(1)} %collective-permute-done.4.b1p) | copy-start | bytes 1622020
where the time goes:
time: 77.8 us; the launch traced here: 76.9 us
  Pallas kernels  37.9 us (49%)
  starting transfers between devices  25.1 us (32%)
  waiting for transfers between devices  10.5 us (13%)
  local copies, waits for them, and re-layouts  2.66 us (3%)
    ppermute x6, starting transfers between devices, from_partner(): return lax.ppermute(value, 'seq', pairs)  19.8 us
    pallas_call x1, Pallas kernels, shards(): pl.pallas_call(_bwd2_kernel, grid=(heads,), in_specs=[_cols(n0), _cols(n0...  10.9 us
    ppermute x6, waiting for transfers between devices, from_partner(): return lax.ppermute(value, 'seq', pairs)  9.2 us
    pallas_call x1, Pallas kernels, shards(): pl.pallas_call(_fwd12_kernel, grid=(heads,), in_specs=[_cols(n0), _per_he...  6.74 us
    pallas_call x1, Pallas kernels, shards(): pl.pallas_call(_own_kernel, grid=(heads,), in_specs=[_stacked(n1, 0), _st...  6.01 us
    pallas_call x1, Pallas kernels, shards(): pl.pallas_call(_bwd1_kernel, grid=(heads,), in_specs=[_cols(n0), _cols(n0...  5.69 us
    pallas_call x1, Pallas kernels, shards(): pl.pallas_call(_fwd0_kernel, grid=(heads,), in_specs=[_cols(n0), _cols(n0...  5.43 us
    ppermute x1, starting transfers between devices, shards(): other = lax.ppermute(sums, 'head', [(0, 1), (1, 0)])  5.34 us
  transfers between devices with their start and end apart: 7, of which 3 were waited for; matrix products, arithmetic and copies ran while one was open for 0% of the time, Pallas kernels for 21%

commit v1 on v0

--- a/solution.py
+++ b/solution.py
@@ -325,7 +325,12 @@
     r2a = from_partner(s2, 2)
     r2b = from_partner(s2, 3)
 
-    a0, ms0 = pl.pallas_call(
+    a0, ms0 = _fwd0_call(heads, n0, width, q0, k0, v0)
+    return _rest(heads, n0, n1, n2, width, q0, k0, v0, g0, s1, q1, s2, q2, r1, r2a, r2b, a0, ms0)
+
+
+def _fwd0_call(heads, n0, width, q0, k0, v0):
+    return pl.pallas_call(
         _fwd0_kernel,
         grid=(heads,),
         in_specs=[_cols(n0), _cols(n0), _cols(n0)],
@@ -337,6 +342,8 @@
         compiler_params=_params(),
     )(q0, k0, v0)
 
+
+def _rest(heads, n0, n1, n2, width, q0, k0, v0, g0, s1, q1, s2, q2, r1, r2a, r2b, a0, ms0):
     att, w, sums = pl.pallas_call(
         _fwd12_kernel,
         grid=(heads,),

time: 77.8 us -> 77.8 us (level)
  no operation moved by 1% of the time
where the time goes in v1:
time: 77.8 us; the launch traced here: 76.9 us
  Pallas kernels  37.9 us (49%)
  starting transfers between devices  25.1 us (32%)
  waiting for transfers between devices  10.5 us (13%)
  local copies, waits for them, and re-layouts  2.66 us (3%)
    ppermute x6, starting transfers between devices, from_partner(): return lax.ppermute(value, 'seq', pairs)  19.8 us
    pallas_call x1, Pallas kernels, _rest(): pl.pallas_call(_bwd2_kernel, grid=(heads,), in_specs=[_cols(n0), _cols(n0...  10.9 us
    ppermute x6, waiting for transfers between devices, from_partner(): return lax.ppermute(value, 'seq', pairs)  9.2 us
    pallas_call x1, Pallas kernels, _rest(): pl.pallas_call(_fwd12_kernel, grid=(heads,), in_specs=[_cols(n0), _per_he...  6.74 us
    pallas_call x1, Pallas kernels, _rest(): pl.pallas_call(_own_kernel, grid=(heads,), in_specs=[_stacked(n1, 0), _st...  6.01 us
    pallas_call x1, Pallas kernels, _rest(): pl.pallas_call(_bwd1_kernel, grid=(heads,), in_specs=[_cols(n0), _cols(n0...  5.69 us
    pallas_call x1, Pallas kernels, _fwd0_call(): pl.pallas_call(_fwd0_kernel, grid=(heads,), in_specs=[_cols(n0), _cols(n0...  5.43 us
    ppermute x1, starting transfers between devices, _rest(): other = lax.ppermute(sums, 'head', [(0, 1), (1, 0)])  5.34 us
  transfers between devices with their start and end apart: 7, of which 3 were waited for; matrix products, arithmetic and copies ran while one was open for 0% of the time, Pallas kernels for 21%

profile of v1, /device:TPU:1, one launch (start us, length us, event | category | flops | bytes accessed | tf_op | source)
XLA Modules:
  0.0 76.9 jit_solution(14831040571360207991)
XLA Ops:
  0.6 3.1 %shard_map.76 = (bf16[2,256,512]{2,1,0:T(8,128)(2,1)}, bf16[256,512]{1,0:T(8,128)(2,1)}, bf16[2,128,512]{2,1,0:T(8,128)(2,1)}, bf16[128,512]{1,0:T(8,128)(2,1)}) custom-call(bf16[512,512]{1,0:T(8,128)(2,1)} %q0.5, bf16[512,512]{1,0:T(8,128)(2,1)} %k0.5, bf16[512,512]{1,0:T(8,128)(2,1)} %v0.5), custom_call_target="tpu_custom_call" | custom-call | tf_op jit(solution)/shard_map/pallas_call | solution.py:310
  3.7 3.9 %collective-permute-start = (bf16[2,256,512]{2,1,0:T(8,128)(2,1)}, bf16[2,256,512]{2,1,0:T(8,128)(2,1)S(1)}, u32[]{:S(2)}, u32[]{:S(2)}) collective-permute-start(bf16[2,256,512]{2,1,0:T(8,128)(2,1)} %get-tuple-element.24.k1o.v1o), channel_id=1, source_target_pairs={{0,2},{2,0},{4,6},{6,4},{8,10},{10,8},{12,14},{14,12},{16,18},{18,... | collective-permute-start | bytes 1572872 | tf_op jit(solution)/shard_map/ppermute | solution.py:18
  7.7 4.4 %collective-permute-start.1 = (bf16[2,128,512]{2,1,0:T(8,128)(2,1)}, bf16[2,128,512]{2,1,0:T(8,128)(2,1)S(1)}, u32[]{:S(2)}, u32[]{:S(2)}) collective-permute-start(bf16[2,128,512]{2,1,0:T(8,128)(2,1)} %get-tuple-element.26.k2o.v2o), channel_id=1, source_target_pairs={{0,4},{2,6},{4,0},{6,2},{8,12},{10,14},{12,8},{14,10},{16,20},{18,... | collective-permute-start | bytes 786440 | tf_op jit(solution)/shard_map/ppermute | solution.py:18
  12.0 1.9 %collective-permute-start.2 = (bf16[2,128,512]{2,1,0:T(8,128)(2,1)}, bf16[2,128,512]{2,1,0:T(8,128)(2,1)S(1)}, u32[]{:S(2)}, u32[]{:S(2)}) collective-permute-start(bf16[2,128,512]{2,1,0:T(8,128)(2,1)} %get-tuple-element.26.k2o.v2o), channel_id=1, source_target_pairs={{0,6},{2,4},{4,2},{6,0},{8,14},{10,12},{12,10},{14,8},{16,22},{18,... | collective-permute-start | bytes 786440 | tf_op jit(solution)/shard_map/ppermute | solution.py:18
  14.0 5.4 %shard_map.75 = (f32[512,512]{1,0:T(8,128)}, f32[4,512,128]{2,1,0:T(8,128)}) custom-call(bf16[512,512]{1,0:T(8,128)(2,1)} %q0.5, bf16[512,512]{1,0:T(8,128)(2,1)} %k0.5, bf16[512,512]{1,0:T(8,128)(2,1)} %v0.5), custom_call_target="tpu_custom_call" | custom-call | tf_op jit(solution)/shard_map/pallas_call | solution.py:333
  19.4 7.9 %collective-permute-done.1.k2a.v2a = bf16[2,128,512]{2,1,0:T(8,128)(2,1)S(1)} collective-permute-done((bf16[2,128,512]{2,1,0:T(8,128)(2,1)}, bf16[2,128,512]{2,1,0:T(8,128)(2,1)S(1)}, u32[]{:S(2)}, u32[]{:S(2)}) %collective-permute-start.1) | collective-permute-done | bytes 262176 | tf_op jit(solution)/shard_map/ppermute | solution.py:18
  27.3 0.0 copy-start.1
  27.3 0.0 collective-permute-done.2.k2b.v2b
  27.3 0.0 copy-start.2
  27.3 0.0 collective-permute-done.k1p.v1p
  27.3 0.0 copy-start
  27.3 0.7 copy-done.1
  28.0 0.1 copy-done.2
  28.1 0.2 copy-done
  28.3 6.7 %shard_map.77 = (bf16[512,512]{1,0:T(8,128)(2,1)}, f32[4,512,128]{2,1,0:T(8,128)}, f32[512,128]{1,0:T(8,128)}) custom-call(f32[512,512]{1,0:T(8,128)} %get-tuple-element.21.a0, f32[4,512,128]{2,1,0:T(8,128)} %get-tuple-element.22.ms0, bf16[512,512]{1,0:T(8,128)(2,1)} %g0.5, bf16[256,512]{1,0:T(8,128)(2,1)} %get-tuple-element.23.q1, ...), custom_call_target="tpu_custom_call" | custom-call | tf_op jit(solution)/shard_map/pallas_call | solution.py:347
  35.0 5.3 %collective-permute-start.3 = (f32[512,128]{1,0:T(8,128)}, f32[512,128]{1,0:T(8,128)S(1)}, u32[]{:S(2)}, u32[]{:S(2)}) collective-permute-start(f32[512,128]{1,0:T(8,128)} %get-tuple-element.29.mine), channel_id=1, source_target_pairs={{0,1},{1,0},{2,3},{3,2},{4,5},{5,4},{6,7},{7,6},{8,9},{9,8},{10,11... | collective-permute-start | bytes 786440 | tf_op jit(solution)/shard_map/ppermute | solution.py:366
  40.4 1.4 %collective-permute-done.3.theirs = f32[512,128]{1,0:T(8,128)S(1)} collective-permute-done((f32[512,128]{1,0:T(8,128)}, f32[512,128]{1,0:T(8,128)S(1)}, u32[]{:S(2)}, u32[]{:S(2)}) %collective-permute-start.3) | collective-permute-done | bytes 262176 | tf_op jit(solution)/shard_map/ppermute | solution.py:366
  41.7 0.0 copy-start.3
  41.7 0.7 copy-done.3
  42.4 5.7 %shard_map.78 = (bf16[512,512]{1,0:T(8,128)(2,1)}, bf16[528,512]{1,0:T(8,128)(2,1)}, bf16[272,512]{1,0:T(8,128)(2,1)}) custom-call(bf16[512,512]{1,0:T(8,128)(2,1)} %g0.5, bf16[512,512]{1,0:T(8,128)(2,1)} %get-tuple-element.27.att, f32[4,512,128]{2,1,0:T(8,128)} %get-tuple-element.28.w, f32[512,128]{1,0:T(8,128)} %get-tuple-element.29.mine, ...), custom_call_target="tpu_custom_call" | custom-call | tf_op jit(solution)/shard_map/pallas_call | solution.py:368
  48.1 1.9 %collective-permute-start.4 = (bf16[528,512]{1,0:T(8,128)(2,1)}, bf16[528,512]{1,0:T(8,128)(2,1)S(1)}, u32[]{:S(2)}, u32[]{:S(2)}) collective-permute-start(bf16[528,512]{1,0:T(8,128)(2,1)} %get-tuple-element.32), channel_id=1, source_target_pairs={{0,2},{2,0},{4,6},{6,4},{8,10},{10,8},{12,14},{14,12},{16,18},{18,... | collective-permute-start | bytes 1622024 | tf_op jit(solution)/shard_map/ppermute | solution.py:18
  50.1 3.6 %collective-permute-start.5 = (bf16[272,512]{1,0:T(8,128)(2,1)}, bf16[272,512]{1,0:T(8,128)(2,1)S(1)}, u32[]{:S(2)}, u32[]{:S(2)}) collective-permute-start(bf16[272,512]{1,0:T(8,128)(2,1)} %get-tuple-element.33), channel_id=1, source_target_pairs={{0,4},{2,6},{4,0},{6,2},{8,12},{10,14},{12,8},{14,10},{16,20},{18,... | collective-permute-start | bytes 835592 | tf_op jit(solution)/shard_map/ppermute | solution.py:18
  53.6 4.1 %collective-permute-start.6 = (bf16[272,512]{1,0:T(8,128)(2,1)}, bf16[272,512]{1,0:T(8,128)(2,1)S(1)}, u32[]{:S(2)}, u32[]{:S(2)}) collective-permute-start(bf16[272,512]{1,0:T(8,128)(2,1)} %get-tuple-element.33), channel_id=1, source_target_pairs={{0,6},{2,4},{4,2},{6,0},{8,14},{10,12},{12,10},{14,8},{16,22},{18,... | collective-permute-start | bytes 835592 | tf_op jit(solution)/shard_map/ppermute | solution.py:18
  57.7 10.9 %shard_map.79 = (bf16[512,512]{1,0:T(8,128)(2,1)}, f32[512,512]{1,0:T(8,128)}, f32[512,512]{1,0:T(8,128)}) custom-call(bf16[512,512]{1,0:T(8,128)(2,1)} %q0.5, bf16[512,512]{1,0:T(8,128)(2,1)} %k0.5, bf16[512,512]{1,0:T(8,128)(2,1)} %v0.5, bf16[512,512]{1,0:T(8,128)(2,1)} %g0.5, bf16[512,512]{1,0:T(8,128)(2,1)} %get-tuple-element.27.att, ...), custom_call_target="tpu_custom_call" | custom-call | tf_op jit(solution)/shard_map/pallas_call | solution.py:385
  68.6 1.3 %collective-permute-done.5.b2a = bf16[272,512]{1,0:T(8,128)(2,1)S(1)} collective-permute-done((bf16[272,512]{1,0:T(8,128)(2,1)}, bf16[272,512]{1,0:T(8,128)(2,1)S(1)}, u32[]{:S(2)}, u32[]{:S(2)}) %collective-permute-start.5) | collective-permute-done | bytes 278560 | tf_op jit(solution)/shard_map/ppermute | solution.py:18
  69.9 0.0 copy-start.5
  69.9 0.0 collective-permute-done.6.b2b
  69.9 0.0 copy-start.6
  69.9 0.0 collective-permute-done.4.b1p
  69.9 0.0 copy-start.4
  69.9 0.7 copy-done.5
  70.6 0.1 copy-done.6
  70.7 0.2 copy-done.4
  70.9 6.0 %shard_map.80 = (bf16[512,512]{1,0:T(8,128)(2,1)}, bf16[512,512]{1,0:T(8,128)(2,1)}) custom-call(bf16[2,256,512]{2,1,0:T(8,128)(2,1)} %get-tuple-element.24.k1o.v1o, bf16[2,256,512]{2,1,0:T(8,128)(2,1)} %get-tuple-element.24.k1o.v1o, bf16[2,256,512]{2,1,0:T(8,128)(2,1)} %copy-done, bf16[528,512]{1,0:T(8,128)(2,1)} %copy-done.4, ...), custom_call_target="tpu_custom_call" | custom-call | tf_op jit(solution)/shard_map/pallas_call | solution.py:404
Async XLA Ops:
  3.7 23.6 %collective-permute-start = (bf16[2,256,512]{2,1,0:T(8,128)(2,1)}, bf16[2,256,512]{2,1,0:T(8,128)(2,1)S(1)}, u32[]{:S(2)}, u32[]{:S(2)}) collective-permute-start(bf16[2,256,512]{2,1,0:T(8,128)(2,1)} %get-tuple-element.24.k1o.v1o), channel_id=1, source_target_pairs={{0,2},{2,0},{4,6},{6,4},{8,10},{10,8},{12,14},{14,12},{16,18},{18,... | collective-permute-start | bytes 1572872 | tf_op jit(solution)/shard_map/ppermute | solution.py:18
  7.7 19.6 %collective-permute-start.1 = (bf16[2,128,512]{2,1,0:T(8,128)(2,1)}, bf16[2,128,512]{2,1,0:T(8,128)(2,1)S(1)}, u32[]{:S(2)}, u32[]{:S(2)}) collective-permute-start(bf16[2,128,512]{2,1,0:T(8,128)(2,1)} %get-tuple-element.26.k2o.v2o), channel_id=1, source_target_pairs={{0,4},{2,6},{4,0},{6,2},{8,12},{10,14},{12,8},{14,10},{16,20},{18,... | collective-permute-start | bytes 786440 | tf_op jit(solution)/shard_map/ppermute | solution.py:18
  12.0 15.3 %collective-permute-start.2 = (bf16[2,128,512]{2,1,0:T(8,128)(2,1)}, bf16[2,128,512]{2,1,0:T(8,128)(2,1)S(1)}, u32[]{:S(2)}, u32[]{:S(2)}) collective-permute-start(bf16[2,128,512]{2,1,0:T(8,128)(2,1)} %get-tuple-element.26.k2o.v2o), channel_id=1, source_target_pairs={{0,6},{2,4},{4,2},{6,0},{8,14},{10,12},{12,10},{14,8},{16,22},{18,... | collective-permute-start | bytes 786440 | tf_op jit(solution)/shard_map/ppermute | solution.py:18
  27.3 0.7 copy-start.1
  27.3 0.8 %copy-start.2 = (bf16[2,128,512]{2,1,0:T(8,128)(2,1)}, bf16[2,128,512]{2,1,0:T(8,128)(2,1)S(1)}, u32[]{:S(2)}) copy-start(bf16[2,128,512]{2,1,0:T(8,128)(2,1)S(1)} %collective-permute-done.2.k2b.v2b) | copy-start | bytes 786436
  27.3 1.0 %copy-start = (bf16[2,256,512]{2,1,0:T(8,128)(2,1)}, bf16[2,256,512]{2,1,0:T(8,128)(2,1)S(1)}, u32[]{:S(2)}) copy-start(bf16[2,256,512]{2,1,0:T(8,128)(2,1)S(1)} %collective-permute-done.k1p.v1p) | copy-start | bytes 1572868
  35.0 6.7 %collective-permute-start.3 = (f32[512,128]{1,0:T(8,128)}, f32[512,128]{1,0:T(8,128)S(1)}, u32[]{:S(2)}, u32[]{:S(2)}) collective-permute-start(f32[512,128]{1,0:T(8,128)} %get-tuple-element.29.mine), channel_id=1, source_target_pairs={{0,1},{1,0},{2,3},{3,2},{4,5},{5,4},{6,7},{7,6},{8,9},{9,8},{10,11... | collective-permute-start | bytes 786440 | tf_op jit(solution)/shard_map/ppermute | solution.py:366
  41.7 0.7 copy-start.3
  48.1 21.8 %collective-permute-start.4 = (bf16[528,512]{1,0:T(8,128)(2,1)}, bf16[528,512]{1,0:T(8,128)(2,1)S(1)}, u32[]{:S(2)}, u32[]{:S(2)}) collective-permute-start(bf16[528,512]{1,0:T(8,128)(2,1)} %get-tuple-element.32), channel_id=1, source_target_pairs={{0,2},{2,0},{4,6},{6,4},{8,10},{10,8},{12,14},{14,12},{16,18},{18,... | collective-permute-start | bytes 1622024 | tf_op jit(solution)/shard_map/ppermute | solution.py:18
  50.1 19.9 %collective-permute-start.5 = (bf16[272,512]{1,0:T(8,128)(2,1)}, bf16[272,512]{1,0:T(8,128)(2,1)S(1)}, u32[]{:S(2)}, u32[]{:S(2)}) collective-permute-start(bf16[272,512]{1,0:T(8,128)(2,1)} %get-tuple-element.33), channel_id=1, source_target_pairs={{0,4},{2,6},{4,0},{6,2},{8,12},{10,14},{12,8},{14,10},{16,20},{18,... | collective-permute-start | bytes 835592 | tf_op jit(solution)/shard_map/ppermute | solution.py:18
  53.6 16.3 %collective-permute-start.6 = (bf16[272,512]{1,0:T(8,128)(2,1)}, bf16[272,512]{1,0:T(8,128)(2,1)S(1)}, u32[]{:S(2)}, u32[]{:S(2)}) collective-permute-start(bf16[272,512]{1,0:T(8,128)(2,1)} %get-tuple-element.33), channel_id=1, source_target_pairs={{0,6},{2,4},{4,2},{6,0},{8,14},{10,12},{12,10},{14,8},{16,22},{18,... | collective-permute-start | bytes 835592 | tf_op jit(solution)/shard_map/ppermute | solution.py:18
  69.9 0.7 copy-start.5
  69.9 0.8 %copy-start.6 = (bf16[272,512]{1,0:T(8,128)(2,1)}, bf16[272,512]{1,0:T(8,128)(2,1)S(1)}, u32[]{:S(2)}) copy-start(bf16[272,512]{1,0:T(8,128)(2,1)S(1)} %collective-permute-done.6.b2b) | copy-start | bytes 835588
  69.9 1.0 %copy-start.4 = (bf16[528,512]{1,0:T(8,128)(2,1)}, bf16[528,512]{1,0:T(8,128)(2,1)S(1)}, u32[]{:S(2)}) copy-start(bf16[528,512]{1,0:T(8,128)(2,1)S(1)} %collective-permute-done.4.b1p) | copy-start | bytes 1622020
